TPU v7x, 32 devices: a whole 2x2x4 slice. The times are simulated.
32 devices in a mesh: tm: 8 (over z, x), state: 4 (over y, core).
Axes of the slice: x: 2, y: 2, z: 4, core: 2. Of those that a mesh axis runs over, the one named last changes fastest.
Arguments:
- obs: bfloat16 [2048, 16, 256], P(('state', 'tm')), may hold values from -6 to 6
- mask: int32 [2048, 16], P(('state', 'tm')), may hold values 0 or 1
- loadings: bfloat16 [2048, 2048], P('state'), may hold values from -0.125 to 0.125
- decay: float32 [16, 2048], P('tm', 'state'), may hold values from 0 to 1, as said below
Outputs:
- smoothed: float32 [2048, 16, 256], P('state', 'tm')
- residual: float32 [2048, 16, 256], P('state', 'tm')
Inputs may be any that keep to these rules, and one draw needn't show every extreme that they name: Every decay lies strictly between 0 and 1.
All inputs are finite; a program needn't handle non-finite values. No bound on the sum of `mask` on one device may be relied on, other than what follows from the above.
Results may differ from a plain program's by a relative error of at most 0.0021.
Values may be sent and summed in bfloat16 or wider, within the bound.
No kernel may reach another device: no remote copies, remote signals or barrier semaphores. Data moves between devices by JAX's collectives and lax.ppermute only.
A program may use at most 64 MiB of HBM per device.

v0:
```python
import jax
import jax.numpy as jnp
from jax import lax
from jax.sharding import PartitionSpec as P

CHUNKS = 2


def smooth_chunk(information, decay_all):
    comps, hours, width = information.shape
    state = jnp.zeros((comps, width), jnp.float32)
    filtered = []
    for hour in range(hours):
        state = decay_all[hour][:, None] * state + information[:, hour, :]
        filtered.append(state)
    state = jnp.zeros((comps, width), jnp.float32)
    rows = [None] * hours
    for hour in reversed(range(hours)):
        rate = decay_all[hour]
        state = rate[:, None] * state + (1.0 - rate * rate)[:, None] * filtered[hour]
        rows[hour] = state
    return jnp.stack(rows, axis=1)


def local(obs, mask, loadings, decay):
    tm_count = lax.axis_size("tm")
    tm_index = lax.axis_index("tm")
    _, hours, members = obs.shape
    chunk_members = members // CHUNKS
    masked = obs * mask[:, :, None].astype(obs.dtype)
    by_hour = lax.all_to_all(masked, "tm", split_axis=1, concat_axis=0, tiled=True)
    slab_hours, comps = decay.shape
    padded = jnp.zeros((tm_count, slab_hours, comps), jnp.float32)
    padded = lax.dynamic_update_slice(padded, decay[None], (tm_index, 0, 0))
    decay_all = lax.psum(padded, "tm").reshape(tm_count * slab_hours, comps)
    smoothed_parts = []
    residual_parts = []
    for chunk in range(CHUNKS):
        low = chunk * chunk_members
        piece = masked[:, :, low : low + chunk_members]
        by_member = lax.all_to_all(piece, "tm", split_axis=2, concat_axis=0, tiled=True)
        stations_here, _, width = by_member.shape
        partial = jnp.dot(
            loadings.T,
            by_member.reshape(stations_here, hours * width),
            preferred_element_type=jnp.float32,
        )
        information = lax.psum_scatter(partial, "state", scatter_dimension=0, tiled=True)
        information = information.reshape(information.shape[0], hours, width)
        smoothed_here = smooth_chunk(information, decay_all)
        smoothed = lax.all_to_all(smoothed_here, "tm", split_axis=1, concat_axis=2, tiled=True)
        rounded = smoothed.astype(jnp.bfloat16)
        fitted = jnp.einsum(
            "so,ogy->sgy",
            loadings,
            lax.all_gather(rounded, "state", axis=0, tiled=True),
            preferred_element_type=jnp.float32,
        )
        residual = by_hour[:, :, low : low + chunk_members].astype(jnp.float32) - fitted
        smoothed_parts.append(smoothed)
        residual_parts.append(residual)
    return (jnp.concatenate(smoothed_parts, axis=2), jnp.concatenate(residual_parts, axis=2))


def solution(mesh):
    return jax.shard_map(
        local,
        mesh=mesh,
        in_specs=(
            P(("state", "tm"), None, None),
            P(("state", "tm"), None),
            P("state", None),
            P("tm", "state"),
        ),
        out_specs=(P("state", "tm", None), P("state", "tm", None)),
        check_vma=False,
    )
```

profile of v0, /device:TPU:0, one launch (start us, length us, event | category | flops | bytes accessed | tf_op | source)
XLA Modules:
  0.0 196.1 jit_solution(5214605081453235125)
XLA Ops:
  8.1 3.5 %copy.34 = bf16[64,16,256]{0,1,2:T(8,128)(2,1)} copy(bf16[64,16,256]{2,1,0:T(8,128)(2,1)} %param.4) | data formatting | bytes 1048576 | tf_op args[0]
  14.0 1.4 reshape.7069
  15.5 16.1 %all_to_all.84 = bf16[8,2,8192]{2,1,0:T(2,128)(2,1)} all-to-all(bf16[8,2,8192]{2,1,0:T(2,128)(2,1)S(1)} %reshape.7069), channel_id=1, replica_groups=mesh['tm'=8,'state'=4] {'tm'}, dimensions={0} | all-to-all | bytes 524288 | tf_op jit(solution)/shard_map/all_to_all | solution.py:41
  31.6 2.1 %reshape.7070 = bf16[128,16,64]{2,1,0:T(8,128)(2,1)} reshape(bf16[8,2,8192]{2,1,0:T(2,128)(2,1)} %all_to_all.84) | data formatting | bytes 524288
  33.7 2.2 %copy.39 = bf16[8,64,16,16]{1,0,3,2:T(8,128)(2,1)} copy(bf16[8,64,16,16]{1,2,3,0:T(8,128)(2,1)} %bitcast.86) | data formatting | bytes 524288 | tf_op jit(solution)/shard_map/all_to_all | solution.py:41
  37.2 2.0 %convolution_bitcast_fusion = f32[2048,256]{0,1:T(8,128)} fusion(bf16[512,256]{0,1:T(8,128)(2,1)S(1)} %reshape.7066, bf16[512,2048]{1,0:T(8,128)(2,1)S(1)} %copy-done), kind=kOutput, calls=%fused_computation | convolution fusion | flops 536870912 | bytes 4456448 | tf_op jit(solution)/shard_map/dot_general | solution.py:43
  39.4 1.4 reshape.7071
  40.8 12.1 %all_to_all.85 = bf16[8,2,8192]{2,1,0:T(2,128)(2,1)} all-to-all(bf16[8,2,8192]{2,1,0:T(2,128)(2,1)S(1)} %reshape.7071), channel_id=1, replica_groups=mesh['tm'=8,'state'=4] {'tm'}, dimensions={0} | all-to-all | bytes 524288 | tf_op jit(solution)/shard_map/all_to_all | solution.py:41
  52.8 2.1 %reshape.7072 = bf16[128,16,64]{2,1,0:T(8,128)(2,1)} reshape(bf16[8,2,8192]{2,1,0:T(2,128)(2,1)} %all_to_all.85) | data formatting | bytes 524288
  55.0 2.3 %copy.36 = bf16[8,64,16,16]{1,0,3,2:T(8,128)(2,1)} copy(bf16[8,64,16,16]{1,2,3,0:T(8,128)(2,1)} %bitcast.87) | data formatting | bytes 524288 | tf_op jit(solution)/shard_map/all_to_all | solution.py:41
  58.6 2.1 %convolution_bitcast_fusion.1 = f32[2048,256]{0,1:T(8,128)} fusion(bf16[512,256]{0,1:T(8,128)(2,1)S(1)} %reshape.7064, bf16[512,2048]{1,0:T(8,128)(2,1)S(1)} %copy-done), kind=kOutput, calls=%fused_computation.1 | convolution fusion | flops 536870912 | bytes 4456448 | tf_op jit(solution)/shard_map/dot_general | solution.py:43
  61.4 35.2 %psum.7 = f32[16,512]{1,0:T(8,128)S(1)} all-reduce(f32[16,512]{1,0:T(8,128)S(1)} %reshape.7063), channel_id=1, replica_groups=mesh['tm'=8,'state'=4] {'tm'}, use_global_device_ids=true, to_apply=%region_0.0 | all-reduce | flops 8192 | bytes 65536 | tf_op jit(solution)/shard_map/psum | solution.py:35
  101.6 1.9 constant_dynamic-update-slice_fusion.31
  117.0 1.5 constant_dynamic-update-slice_fusion
  118.5 20.1 %all_to_all.86 = f32[512,16,16]{0,2,1:T(8,128)S(1)} all-to-all(f32[512,16,16]{0,2,1:T(8,128)} %get-tuple-element.61), channel_id=1, replica_groups=mesh['tm'=8,'state'=4] {'tm'}, dimensions={1} | all-to-all | bytes 1048576 | tf_op jit(solution)/shard_map/all_to_all | solution.py:51
  140.2 4.2 %all-to-all-start.1 = ((f32[512,16,16]{0,2,1:T(8,128)}), f32[512,16,16]{0,2,1:T(8,128)}, u32[]{:S(2)}, u32[]{:S(2)}) async-start(f32[512,16,16]{0,2,1:T(8,128)} %copy-done.3), calls=%async_computation.2 | async-start | bytes 1048576 | tf_op jit(solution)/shard_map/all_to_all | solution.py:51
  144.3 1.6 copy.41
  146.0 12.1 %all-to-all-done.1 = f32[512,16,16]{0,2,1:T(8,128)} async-done(((f32[512,16,16]{0,2,1:T(8,128)}), f32[512,16,16]{0,2,1:T(8,128)}, u32[]{:S(2)}, u32[]{:S(2)}) %all-to-all-start.1) | async-done | bytes 524320 | tf_op jit(solution)/shard_map/all_to_all | solution.py:51
  158.0 4.1 %all-to-all-start.4 = ((bf16[64,16,256]{2,0,1:T(8,128)(2,1)}), bf16[64,16,256]{2,0,1:T(8,128)(2,1)}, u32[]{:S(2)}, u32[]{:S(2)}) async-start(bf16[64,16,256]{2,0,1:T(8,128)(2,1)} %copy.41), calls=%async_computation.6 | async-start | bytes 1048576 | tf_op jit(solution)/shard_map/all_to_all | solution.py:31
  164.1 11.4 %all-to-all-done.4 = bf16[64,16,256]{2,0,1:T(8,128)(2,1)} async-done(((bf16[64,16,256]{2,0,1:T(8,128)(2,1)}), bf16[64,16,256]{2,0,1:T(8,128)(2,1)}, u32[]{:S(2)}, u32[]{:S(2)}) %all-to-all-start.4) | async-done | bytes 524320 | tf_op jit(solution)/shard_map/all_to_all | solution.py:31
  177.4 1.8 copy.49
  181.1 2.2 %copy.45 = f32[512,2,256]{2,1,0:T(2,128)} copy(f32[512,2,256]{0,2,1:T(8,128)} %pad_maximum_fusion) | data formatting | bytes 2097152
  183.4 2.8 %fusion.13 = f32[512,2,128]{0,2,1:T(8,128)} fusion(bf16[2048,2,128]{0,2,1:T(8,128)(2,1)} %all-gather.5.cloned.1.call-done, bf16[512,2048]{1,0:T(8,128)(2,1)S(1)} %copy-done, bf16[512,2,128]{0,2,1:T(8,128)(2,1)S(1)} %copy-done.6), kind=kOutput, calls=%fused_computation.9 | convolution fusion | flops 537133056 | bytes 3932160 | tf_op jit(solution)/shard_map/so,ogy->sgy/dot_general | solution.py:53
  186.2 2.0 %fusion.7 = f32[512,2,128]{0,2,1:T(8,128)S(1)} fusion(bf16[2048,2,128]{0,2,1:T(8,128)(2,1)} %all-gather.3.cloned.1.call-done, bf16[512,2048]{1,0:T(8,128)(2,1)S(1)} %copy-done, bf16[512,2,128]{0,2,1:T(8,128)(2,1)S(1)} %copy-done.5), kind=kOutput, calls=%fused_computation.7 | convolution fusion | flops 537133056 | bytes 3932160 | tf_op jit(solution)/shard_map/so,ogy->sgy/dot_general | solution.py:53
  (111 shorter events, 33.7 us)
Async XLA Ops:
  7.2 30.1 %copy-start = (bf16[512,2048]{1,0:T(8,128)(2,1)S(1)}, bf16[512,2048]{1,0:T(8,128)(2,1)}, u32[]{:S(2)}) copy-start(bf16[512,2048]{1,0:T(8,128)(2,1)} %param.6) | copy-start | bytes 6291460
  7.2 94.3 %reduce-scatter.5.cloned.1.call-start = ((), (), s32[]{:S(2)}) async-start(), calls=%async_computation.8 | async-start | bytes 2621440 | tf_op jit(solution)/shard_map/reduce_scatter | solution.py:48
  39.3 64.7 %reduce-scatter.3.cloned.1.call-start = ((), (), s32[]{:S(2)}) async-start(), calls=%async_computation.7 | async-start | bytes 2621440 | tf_op jit(solution)/shard_map/reduce_scatter | solution.py:48
  60.7 122.6 %all-gather.5.cloned.1.call-start = ((), (), s32[]{:S(2)}) async-start(), calls=%async_computation.10 | async-start | bytes 1310720 | tf_op jit(solution)/shard_map/all_gather | solution.py:56
  96.6 4.9 %copy-start.7 = (f32[1,512]{1,0:T(1,128)}, f32[1,512]{1,0:T(1,128)S(1)}, u32[]{:S(2)}) copy-start(f32[1,512]{1,0:T(1,128)S(1)} %get-tuple-element.50) | copy-start | bytes 6148
  96.6 4.9 %copy-start.9 = (f32[1,512]{1,0:T(1,128)}, f32[1,512]{1,0:T(1,128)S(1)}, u32[]{:S(2)}) copy-start(f32[1,512]{1,0:T(1,128)S(1)} %get-tuple-element.52) | copy-start | bytes 6148
  96.6 4.9 %copy-start.11 = (f32[1,512]{1,0:T(1,128)}, f32[1,512]{1,0:T(1,128)S(1)}, u32[]{:S(2)}) copy-start(f32[1,512]{1,0:T(1,128)S(1)} %get-tuple-element.54) | copy-start | bytes 6148
  96.7 4.9 %copy-start.12 = (f32[1,512]{1,0:T(1,128)}, f32[1,512]{1,0:T(1,128)S(1)}, u32[]{:S(2)}) copy-start(f32[1,512]{1,0:T(1,128)S(1)} %get-tuple-element.56) | copy-start | bytes 6148
  96.7 4.9 %copy-start.13 = (f32[1,512]{1,0:T(1,128)}, f32[1,512]{1,0:T(1,128)S(1)}, u32[]{:S(2)}) copy-start(f32[1,512]{1,0:T(1,128)S(1)} %get-tuple-element.58) | copy-start | bytes 6148
  96.7 4.9 %copy-start.17 = (f32[1,512]{1,0:T(1,128)}, f32[1,512]{1,0:T(1,128)S(1)}, u32[]{:S(2)}) copy-start(f32[1,512]{1,0:T(1,128)S(1)} %get-tuple-element.47) | copy-start | bytes 6148
  96.7 4.9 %copy-start.18 = (f32[1,512]{1,0:T(1,128)}, f32[1,512]{1,0:T(1,128)S(1)}, u32[]{:S(2)}) copy-start(f32[1,512]{1,0:T(1,128)S(1)} %get-tuple-element.49) | copy-start | bytes 6148
  96.7 4.9 %copy-start.19 = (f32[1,512]{1,0:T(1,128)}, f32[1,512]{1,0:T(1,128)S(1)}, u32[]{:S(2)}) copy-start(f32[1,512]{1,0:T(1,128)S(1)} %get-tuple-element.51) | copy-start | bytes 6148
  96.7 4.9 %copy-start.20 = (f32[1,512]{1,0:T(1,128)}, f32[1,512]{1,0:T(1,128)S(1)}, u32[]{:S(2)}) copy-start(f32[1,512]{1,0:T(1,128)S(1)} %get-tuple-element.53) | copy-start | bytes 6148
  96.7 4.9 %copy-start.21 = (f32[1,512]{1,0:T(1,128)}, f32[1,512]{1,0:T(1,128)S(1)}, u32[]{:S(2)}) copy-start(f32[1,512]{1,0:T(1,128)S(1)} %get-tuple-element.55) | copy-start | bytes 6148
  104.0 7.3 %copy-start.10 = (f32[1,512]{1,0:T(1,128)S(1)}, f32[1,512]{1,0:T(1,128)}, u32[]{:S(2)}) copy-start(f32[1,512]{1,0:T(1,128)} %copy-done.9) | copy-start | bytes 6148
  104.0 7.3 %copy-start.16 = (f32[512]{0:T(512)S(1)}, f32[512]{0:T(512)}, u32[]{:S(2)}) copy-start(f32[512]{0:T(512)} %get-tuple-element.86) | copy-start | bytes 6148
  104.0 8.6 %copy-start.8 = (f32[1,512]{1,0:T(1,128)S(1)}, f32[1,512]{1,0:T(1,128)}, u32[]{:S(2)}) copy-start(f32[1,512]{1,0:T(1,128)} %copy-done.7) | copy-start | bytes 6148
  104.0 8.6 %copy-start.15 = (f32[512]{0:T(512)S(1)}, f32[512]{0:T(512)}, u32[]{:S(2)}) copy-start(f32[512]{0:T(512)} %get-tuple-element.88) | copy-start | bytes 6148
  104.0 9.8 %copy-start.14 = (f32[512]{0:T(512)S(1)}, f32[512]{0:T(512)}, u32[]{:S(2)}) copy-start(f32[512]{0:T(512)} %get-tuple-element.90) | copy-start | bytes 6148
  118.5 20.1 %copy-start.3 = (f32[512,16,16]{0,2,1:T(8,128)}, f32[512,16,16]{0,2,1:T(8,128)S(1)}, u32[]{:S(2)}) copy-start(f32[512,16,16]{0,2,1:T(8,128)S(1)} %get-tuple-element.60) | copy-start | bytes 1572868
  140.2 17.9 %all-to-all-start.1 = ((f32[512,16,16]{0,2,1:T(8,128)}), f32[512,16,16]{0,2,1:T(8,128)}, u32[]{:S(2)}, u32[]{:S(2)}) async-start(f32[512,16,16]{0,2,1:T(8,128)} %copy-done.3), calls=%async_computation.2 | async-start | bytes 1048576 | tf_op jit(solution)/shard_map/all_to_all | solution.py:51
  158.0 17.5 %all-to-all-start.4 = ((bf16[64,16,256]{2,0,1:T(8,128)(2,1)}), bf16[64,16,256]{2,0,1:T(8,128)(2,1)}, u32[]{:S(2)}, u32[]{:S(2)}) async-start(bf16[64,16,256]{2,0,1:T(8,128)(2,1)} %copy.41), calls=%async_computation.6 | async-start | bytes 1048576 | tf_op jit(solution)/shard_map/all_to_all | solution.py:31
  162.2 24.0 %all-gather.3.cloned.1.call-start = ((), (), s32[]{:S(2)}) async-start(), calls=%async_computation.9 | async-start | bytes 1310720 | tf_op jit(solution)/shard_map/all_gather | solution.py:56
  163.3 16.7 %copy-start.2 = (f32[512,8,2,16]{0,3,1,2:T(8,128)S(1)}, f32[512,8,2,16]{0,3,1,2:T(8,128)}, u32[]{:S(2)}) copy-start(f32[512,8,2,16]{0,3,1,2:T(8,128)} %copy-done.1) | copy-start | bytes 1572868
  (7 other events, 19.4 us)
Sparse Core Ops, SparseCore 0:
  39.4 30.4 reduce-scatter.4
  72.6 31.3 reduce-scatter.2
  140.3 14.7 all-gather.4
  164.3 17.0 all-gather.2
where the time goes:
time: 198 us; the launch traced here: 196 us
  blocking collectives  83.4 us (42%)
  local copies, waits for them, and re-layouts  35.7 us (18%)
  waiting for transfers between devices  24.1 us (12%)
  other arithmetic  21.4 us (11%)
  between operations  14.1 us (7%)
  matrix products  8.94 us (5%)
  starting transfers between devices  8.46 us (4%)
    psum x1, blocking collectives, local(): decay_all = lax.psum(padded, 'tm').reshape(tm_count * slab_hours, comps)  35.2 us
    all_to_all x2, blocking collectives, local(): lax.all_to_all(piece, 'tm', split_axis=2, concat_axis=0, tiled=True)  28.1 us
    unnamed x73, local copies, waits for them, and re-layouts  22.7 us
    all_to_all x1, blocking collectives, local(): lax.all_to_all(smoothed_here, 'tm', split_axis=1, concat_axis=2, tiled=True)  20.1 us
    all_to_all x1, waiting for transfers between devices, local(): lax.all_to_all(smoothed_here, 'tm', split_axis=1, concat_axis=2, tiled=True)  12.1 us
    all_to_all x1, waiting for transfers between devices, local(): lax.all_to_all(masked, 'tm', split_axis=1, concat_axis=0, tiled=True)  11.4 us
    unnamed x9, other arithmetic  10.5 us
    dot_general x2, matrix products, local(): jnp.einsum('so,ogy->sgy', loadings, lax.all_gather(rounded, 'state', axis...  4.83 us
  transfers between devices with their start and end apart: 6, of which 3 were waited for; matrix products, arithmetic and copies ran while one was open for 15% of the time, Pallas kernels for 0%

commit v1 on v0

--- a/solution.py
+++ b/solution.py
@@ -32,7 +32,7 @@
     slab_hours, comps = decay.shape
     padded = jnp.zeros((tm_count, slab_hours, comps), jnp.float32)
     padded = lax.dynamic_update_slice(padded, decay[None], (tm_index, 0, 0))
-    decay_all = lax.psum(padded, "tm").reshape(tm_count * slab_hours, comps)
+    decay_all = jnp.sum(lax.all_gather(padded, "tm"), axis=0).reshape(tm_count * slab_hours, comps)
     smoothed_parts = []
     residual_parts = []
     for chunk in range(CHUNKS):

time: 198 us -> 198 us (level)
  blocking collectives: 83.4 us -> 79 us
  waiting for transfers between devices: 24.1 us -> 28.3 us
    psum x1 -> x0, blocking collectives: 35.2 us -> none  [local(): decay_all = lax.psum(padded, 'tm').reshape(tm_count * slab_hours, comps)]
    all_gather x0 -> x1, blocking collectives: none -> 30.8 us  [local(): lax.all_gather(padded, 'tm')]
    reduce_scatter x2, waiting for transfers between devices: 0.49 us -> 4.73 us  [local(): lax.psum_scatter(partial, 'state', scatter_dimension=0, tiled=True)]
where the time goes in v1:
time: 198 us; the launch traced here: 196 us
  blocking collectives  79 us (40%)
  local copies, waits for them, and re-layouts  35.8 us (18%)
  waiting for transfers between devices  28.3 us (14%)
  other arithmetic  21.5 us (11%)
  between operations  14.1 us (7%)
  matrix products  8.94 us (5%)
  starting transfers between devices  8.46 us (4%)
    all_gather x1, blocking collectives, local(): lax.all_gather(padded, 'tm')  30.8 us
    all_to_all x2, blocking collectives, local(): lax.all_to_all(piece, 'tm', split_axis=2, concat_axis=0, tiled=True)  28.1 us
    unnamed x73, local copies, waits for them, and re-layouts  22.7 us
    all_to_all x1, blocking collectives, local(): lax.all_to_all(smoothed_here, 'tm', split_axis=1, concat_axis=2, tiled=True)  20.1 us
    all_to_all x1, waiting for transfers between devices, local(): lax.all_to_all(smoothed_here, 'tm', split_axis=1, concat_axis=2, tiled=True)  12.1 us
    all_to_all x1, waiting for transfers between devices, local(): lax.all_to_all(masked, 'tm', split_axis=1, concat_axis=0, tiled=True)  11.4 us
    unnamed x9, other arithmetic  10.5 us
    dot_general x2, matrix products, local(): jnp.einsum('so,ogy->sgy', loadings, lax.all_gather(rounded, 'state', axis...  4.83 us
  transfers between devices with their start and end apart: 6, of which 3 were waited for; matrix products, arithmetic and copies ran while one was open for 15% of the time, Pallas kernels for 0%

profile of v1, /device:TPU:0, one launch (start us, length us, event | category | flops | bytes accessed | tf_op | source)
XLA Modules:
  0.0 196.1 jit_solution(8259506804306454687)
XLA Ops:
  8.1 3.5 %copy.61 = bf16[64,16,256]{0,1,2:T(8,128)(2,1)} copy(bf16[64,16,256]{2,1,0:T(8,128)(2,1)} %param.4) | data formatting | bytes 1048576 | tf_op args[0]
  15.5 16.1 %all_to_all.84 = bf16[8,2,8192]{2,1,0:T(2,128)(2,1)} all-to-all(bf16[8,2,8192]{2,1,0:T(2,128)(2,1)S(1)} %reshape.7072), channel_id=1, replica_groups=mesh['tm'=8,'state'=4] {'tm'}, dimensions={0} | all-to-all | bytes 524288 | tf_op jit(solution)/shard_map/all_to_all | solution.py:41
  31.6 2.1 %reshape.7073 = bf16[128,16,64]{2,1,0:T(8,128)(2,1)} reshape(bf16[8,2,8192]{2,1,0:T(2,128)(2,1)} %all_to_all.84) | data formatting | bytes 524288
  33.7 2.2 %copy.66 = bf16[8,64,16,16]{1,0,3,2:T(8,128)(2,1)} copy(bf16[8,64,16,16]{1,2,3,0:T(8,128)(2,1)} %bitcast.84) | data formatting | bytes 524288 | tf_op jit(solution)/shard_map/all_to_all | solution.py:41
  37.2 2.0 %convolution_bitcast_fusion = f32[2048,256]{0,1:T(8,128)} fusion(bf16[512,256]{0,1:T(8,128)(2,1)S(1)} %reshape.7069, bf16[512,2048]{1,0:T(8,128)(2,1)S(1)} %copy-done), kind=kOutput, calls=%fused_computation | convolution fusion | flops 536870912 | bytes 4456448 | tf_op jit(solution)/shard_map/dot_general | solution.py:43
  39.4 1.4 reshape.7074
  40.8 12.1 %all_to_all.85 = bf16[8,2,8192]{2,1,0:T(2,128)(2,1)} all-to-all(bf16[8,2,8192]{2,1,0:T(2,128)(2,1)S(1)} %reshape.7074), channel_id=1, replica_groups=mesh['tm'=8,'state'=4] {'tm'}, dimensions={0} | all-to-all | bytes 524288 | tf_op jit(solution)/shard_map/all_to_all | solution.py:41
  52.8 2.1 %reshape.7075 = bf16[128,16,64]{2,1,0:T(8,128)(2,1)} reshape(bf16[8,2,8192]{2,1,0:T(2,128)(2,1)} %all_to_all.85) | data formatting | bytes 524288
  55.0 2.3 %copy.63 = bf16[8,64,16,16]{1,0,3,2:T(8,128)(2,1)} copy(bf16[8,64,16,16]{1,2,3,0:T(8,128)(2,1)} %bitcast.85) | data formatting | bytes 524288 | tf_op jit(solution)/shard_map/all_to_all | solution.py:41
  58.6 2.1 %convolution_bitcast_fusion.1 = f32[2048,256]{0,1:T(8,128)} fusion(bf16[512,256]{0,1:T(8,128)(2,1)S(1)} %reshape.7067, bf16[512,2048]{1,0:T(8,128)(2,1)S(1)} %copy-done), kind=kOutput, calls=%fused_computation.1 | convolution fusion | flops 536870912 | bytes 4456448 | tf_op jit(solution)/shard_map/dot_general | solution.py:43
  61.5 30.8 %all_gather.13 = f32[8,8,2,512]{3,1,2,0:T(8,128)S(1)} all-gather(f32[1,8,2,512]{3,1,2,0:T(8,128)S(1)} %dynamic_update_slice.4), channel_id=1, replica_groups=mesh['tm'=8,'state'=4] {'tm'}, dimensions={0}, use_global_device_ids=true | all-gather | bytes 294912 | tf_op jit(solution)/shard_map/all_gather | solution.py:35
  97.4 1.9 constant_dynamic-update-slice_fusion.31
  99.3 4.7 %reduce-scatter.3.cloned.1.call-done = f32[512,256]{0,1:T(8,128)} async-done(((f32[2048,256]{0,1:T(8,128)}), f32[512,256]{0,1:T(8,128)}) %reduce-scatter.3.cloned.1.call-update) | async-done | bytes 524304 | tf_op jit(solution)/shard_map/reduce_scatter | solution.py:48
  117.0 1.5 constant_dynamic-update-slice_fusion
  118.5 20.1 %all_to_all.86 = f32[512,16,16]{0,2,1:T(8,128)S(1)} all-to-all(f32[512,16,16]{0,2,1:T(8,128)} %get-tuple-element.65), channel_id=1, replica_groups=mesh['tm'=8,'state'=4] {'tm'}, dimensions={1} | all-to-all | bytes 1048576 | tf_op jit(solution)/shard_map/all_to_all | solution.py:51
  140.2 4.2 %all-to-all-start.1 = ((f32[512,16,16]{0,2,1:T(8,128)}), f32[512,16,16]{0,2,1:T(8,128)}, u32[]{:S(2)}, u32[]{:S(2)}) async-start(f32[512,16,16]{0,2,1:T(8,128)} %copy-done.3), calls=%async_computation.2 | async-start | bytes 1048576 | tf_op jit(solution)/shard_map/all_to_all | solution.py:51
  144.3 1.6 copy.68
  146.0 12.1 %all-to-all-done.1 = f32[512,16,16]{0,2,1:T(8,128)} async-done(((f32[512,16,16]{0,2,1:T(8,128)}), f32[512,16,16]{0,2,1:T(8,128)}, u32[]{:S(2)}, u32[]{:S(2)}) %all-to-all-start.1) | async-done | bytes 524320 | tf_op jit(solution)/shard_map/all_to_all | solution.py:51
  158.0 4.1 %all-to-all-start.4 = ((bf16[64,16,256]{2,0,1:T(8,128)(2,1)}), bf16[64,16,256]{2,0,1:T(8,128)(2,1)}, u32[]{:S(2)}, u32[]{:S(2)}) async-start(bf16[64,16,256]{2,0,1:T(8,128)(2,1)} %copy.68), calls=%async_computation.6 | async-start | bytes 1048576 | tf_op jit(solution)/shard_map/all_to_all | solution.py:31
  164.1 11.4 %all-to-all-done.4 = bf16[64,16,256]{2,0,1:T(8,128)(2,1)} async-done(((bf16[64,16,256]{2,0,1:T(8,128)(2,1)}), bf16[64,16,256]{2,0,1:T(8,128)(2,1)}, u32[]{:S(2)}, u32[]{:S(2)}) %all-to-all-start.4) | async-done | bytes 524320 | tf_op jit(solution)/shard_map/all_to_all | solution.py:31
  177.4 1.8 copy.76
  181.1 2.2 %copy.72 = f32[512,2,256]{2,1,0:T(2,128)} copy(f32[512,2,256]{0,2,1:T(8,128)} %pad_maximum_fusion) | data formatting | bytes 2097152
  183.4 2.8 %fusion.13 = f32[512,2,128]{0,2,1:T(8,128)} fusion(bf16[2048,2,128]{0,2,1:T(8,128)(2,1)} %all-gather.5.cloned.1.call-done, bf16[512,2048]{1,0:T(8,128)(2,1)S(1)} %copy-done, bf16[512,2,128]{0,2,1:T(8,128)(2,1)S(1)} %copy-done.6), kind=kOutput, calls=%fused_computation.9 | convolution fusion | flops 537133056 | bytes 3932160 | tf_op jit(solution)/shard_map/so,ogy->sgy/dot_general | solution.py:53
  186.2 2.0 %fusion.7 = f32[512,2,128]{0,2,1:T(8,128)S(1)} fusion(bf16[2048,2,128]{0,2,1:T(8,128)(2,1)} %all-gather.3.cloned.1.call-done, bf16[512,2048]{1,0:T(8,128)(2,1)S(1)} %copy-done, bf16[512,2,128]{0,2,1:T(8,128)(2,1)S(1)} %copy-done.5), kind=kOutput, calls=%fused_computation.7 | convolution fusion | flops 537133056 | bytes 3932160 | tf_op jit(solution)/shard_map/so,ogy->sgy/dot_general | solution.py:53
  (114 shorter events, 34.8 us)
Async XLA Ops:
  7.2 30.1 %copy-start = (bf16[512,2048]{1,0:T(8,128)(2,1)S(1)}, bf16[512,2048]{1,0:T(8,128)(2,1)}, u32[]{:S(2)}) copy-start(bf16[512,2048]{1,0:T(8,128)(2,1)} %param.6) | copy-start | bytes 6291460
  7.2 90.1 %reduce-scatter.5.cloned.1.call-start = ((), (), s32[]{:S(2)}) async-start(), calls=%async_computation.8 | async-start | bytes 2621440 | tf_op jit(solution)/shard_map/reduce_scatter | solution.py:48
  39.3 64.7 %reduce-scatter.3.cloned.1.call-start = ((), (), s32[]{:S(2)}) async-start(), calls=%async_computation.7 | async-start | bytes 2621440 | tf_op jit(solution)/shard_map/reduce_scatter | solution.py:48
  60.7 122.6 %all-gather.5.cloned.1.call-start = ((), (), s32[]{:S(2)}) async-start(), calls=%async_computation.10 | async-start | bytes 1310720 | tf_op jit(solution)/shard_map/all_gather | solution.py:56
  92.4 4.9 %copy-start.7 = (f32[1,512]{1,0:T(1,128)}, f32[1,512]{1,0:T(1,128)S(1)}, u32[]{:S(2)}) copy-start(f32[1,512]{1,0:T(1,128)S(1)} %get-tuple-element.54) | copy-start | bytes 6148
  92.4 4.9 %copy-start.9 = (f32[1,512]{1,0:T(1,128)}, f32[1,512]{1,0:T(1,128)S(1)}, u32[]{:S(2)}) copy-start(f32[1,512]{1,0:T(1,128)S(1)} %get-tuple-element.56) | copy-start | bytes 6148
  92.4 4.9 %copy-start.11 = (f32[1,512]{1,0:T(1,128)}, f32[1,512]{1,0:T(1,128)S(1)}, u32[]{:S(2)}) copy-start(f32[1,512]{1,0:T(1,128)S(1)} %get-tuple-element.58) | copy-start | bytes 6148
  92.4 4.9 %copy-start.12 = (f32[1,512]{1,0:T(1,128)}, f32[1,512]{1,0:T(1,128)S(1)}, u32[]{:S(2)}) copy-start(f32[1,512]{1,0:T(1,128)S(1)} %get-tuple-element.60) | copy-start | bytes 6148
  92.4 4.9 %copy-start.13 = (f32[1,512]{1,0:T(1,128)}, f32[1,512]{1,0:T(1,128)S(1)}, u32[]{:S(2)}) copy-start(f32[1,512]{1,0:T(1,128)S(1)} %get-tuple-element.62) | copy-start | bytes 6148
  92.4 4.9 %copy-start.17 = (f32[1,512]{1,0:T(1,128)}, f32[1,512]{1,0:T(1,128)S(1)}, u32[]{:S(2)}) copy-start(f32[1,512]{1,0:T(1,128)S(1)} %get-tuple-element.51) | copy-start | bytes 6148
  92.4 4.9 %copy-start.18 = (f32[1,512]{1,0:T(1,128)}, f32[1,512]{1,0:T(1,128)S(1)}, u32[]{:S(2)}) copy-start(f32[1,512]{1,0:T(1,128)S(1)} %get-tuple-element.53) | copy-start | bytes 6148
  92.5 4.9 %copy-start.19 = (f32[1,512]{1,0:T(1,128)}, f32[1,512]{1,0:T(1,128)S(1)}, u32[]{:S(2)}) copy-start(f32[1,512]{1,0:T(1,128)S(1)} %get-tuple-element.55) | copy-start | bytes 6148
  92.5 4.9 %copy-start.20 = (f32[1,512]{1,0:T(1,128)}, f32[1,512]{1,0:T(1,128)S(1)}, u32[]{:S(2)}) copy-start(f32[1,512]{1,0:T(1,128)S(1)} %get-tuple-element.57) | copy-start | bytes 6148
  92.5 4.9 %copy-start.21 = (f32[1,512]{1,0:T(1,128)}, f32[1,512]{1,0:T(1,128)S(1)}, u32[]{:S(2)}) copy-start(f32[1,512]{1,0:T(1,128)S(1)} %get-tuple-element.59) | copy-start | bytes 6148
  104.0 7.3 %copy-start.10 = (f32[1,512]{1,0:T(1,128)S(1)}, f32[1,512]{1,0:T(1,128)}, u32[]{:S(2)}) copy-start(f32[1,512]{1,0:T(1,128)} %copy-done.9) | copy-start | bytes 6148
  104.0 7.3 %copy-start.16 = (f32[512]{0:T(512)S(1)}, f32[512]{0:T(512)}, u32[]{:S(2)}) copy-start(f32[512]{0:T(512)} %get-tuple-element.90) | copy-start | bytes 6148
  104.0 8.6 %copy-start.8 = (f32[1,512]{1,0:T(1,128)S(1)}, f32[1,512]{1,0:T(1,128)}, u32[]{:S(2)}) copy-start(f32[1,512]{1,0:T(1,128)} %copy-done.7) | copy-start | bytes 6148
  104.0 8.6 %copy-start.15 = (f32[512]{0:T(512)S(1)}, f32[512]{0:T(512)}, u32[]{:S(2)}) copy-start(f32[512]{0:T(512)} %get-tuple-element.92) | copy-start | bytes 6148
  104.0 9.8 %copy-start.14 = (f32[512]{0:T(512)S(1)}, f32[512]{0:T(512)}, u32[]{:S(2)}) copy-start(f32[512]{0:T(512)} %get-tuple-element.94) | copy-start | bytes 6148
  118.5 20.1 %copy-start.3 = (f32[512,16,16]{0,2,1:T(8,128)}, f32[512,16,16]{0,2,1:T(8,128)S(1)}, u32[]{:S(2)}) copy-start(f32[512,16,16]{0,2,1:T(8,128)S(1)} %get-tuple-element.64) | copy-start | bytes 1572868
  140.2 17.9 %all-to-all-start.1 = ((f32[512,16,16]{0,2,1:T(8,128)}), f32[512,16,16]{0,2,1:T(8,128)}, u32[]{:S(2)}, u32[]{:S(2)}) async-start(f32[512,16,16]{0,2,1:T(8,128)} %copy-done.3), calls=%async_computation.2 | async-start | bytes 1048576 | tf_op jit(solution)/shard_map/all_to_all | solution.py:51
  158.0 17.5 %all-to-all-start.4 = ((bf16[64,16,256]{2,0,1:T(8,128)(2,1)}), bf16[64,16,256]{2,0,1:T(8,128)(2,1)}, u32[]{:S(2)}, u32[]{:S(2)}) async-start(bf16[64,16,256]{2,0,1:T(8,128)(2,1)} %copy.68), calls=%async_computation.6 | async-start | bytes 1048576 | tf_op jit(solution)/shard_map/all_to_all | solution.py:31
  162.2 24.0 %all-gather.3.cloned.1.call-start = ((), (), s32[]{:S(2)}) async-start(), calls=%async_computation.9 | async-start | bytes 1310720 | tf_op jit(solution)/shard_map/all_gather | solution.py:56
  163.3 16.7 %copy-start.2 = (f32[512,8,2,16]{0,3,1,2:T(8,128)S(1)}, f32[512,8,2,16]{0,3,1,2:T(8,128)}, u32[]{:S(2)}) copy-start(f32[512,8,2,16]{0,3,1,2:T(8,128)} %copy-done.1) | copy-start | bytes 1572868
  (7 other events, 19.4 us)
Sparse Core Ops, SparseCore 0:
  39.4 30.4 reduce-scatter.4
  72.6 31.3 reduce-scatter.2
  140.3 14.7 all-gather.4
  164.3 17.0 all-gather.2
